TPU v7x, 32 devices: a whole 2x2x4 slice. The times are simulated.
32 devices in a mesh: groups: 2 (over y), blk: 4 (over z), pool: 4 (over x, core).
Axes of the slice: x: 2, y: 2, z: 4, core: 2. Of those that a mesh axis runs over, the one named last changes fastest.
Arguments:
- q_new: bfloat16 [1024, 8192], P(('groups', 'blk'), 'pool'), parts along dimension 0, may hold values from -64 to 64
- kv_new: bfloat16 [1024, 8, 256], P(('groups', 'blk'), 'pool'), parts along dimension 0, may hold values from -7 to 7
- kv_cache: bfloat16 [256, 8, 128, 256], P(('groups', 'blk'), 'pool'), parts along dimension 0, may hold values from -4.5 to 4.5
- page_table: int32 [16], P('groups'), parts along dimension 0, may hold values from 0 to 127, as said below
- block_offsets: int32 [8], P('groups'), parts along dimension 0, may hold values from 0 to 3, each once
Outputs:
- attended: bfloat16 [1024, 8192], P(('groups', 'blk'), 'pool'), parts along dimension 0
There are 2 independent parts, one for each index of `groups`. A program takes and returns all parts, laid end to end along the dimension named above; each array names one. Nothing has to cross between parts.
Inputs may be any that keep to these rules, and one draw needn't show every extreme that they name: `page_table`: distinct slots; slot s lies on blk index s // 32; at most 4 entries lie on the slots of one blk index, and exactly 4 on some blk index.
All inputs are finite; a program needn't handle non-finite values.
Results may differ from a plain program's by a relative error of at most 0.0045.
Values may be sent and summed in bfloat16 or wider, within the bound.
No kernel may reach another device: no remote copies, remote signals or barrier semaphores. Data moves between devices by JAX's collectives and lax.ppermute only.
A program may use at most 64 MiB of HBM per device.

v0:
```python
import math
import jax
import jax.numpy as jnp
from jax import lax
from jax.sharding import PartitionSpec as P

CAP = 4


def attend(running, queries, keys, values, visible, head_size):
    maxima, totals, summed = running
    score_scale = 1.0 / math.sqrt(head_size)
    scores = (
        jnp.einsum("gqd,gkd->gqk", queries, keys, preferred_element_type=jnp.float32) * score_scale
    )
    scores = jnp.where(visible, scores, -1e30)
    row_top = jnp.maximum(maxima, jnp.max(scores, axis=2))
    factor = jnp.exp(maxima - row_top)
    weights = jnp.where(visible, jnp.exp(scores - row_top[..., None]), 0.0)
    totals = totals * factor + jnp.sum(weights, axis=2)
    summed = summed * factor[..., None] + jnp.einsum(
        "gqk,gkd->gqd", weights.astype(jnp.bfloat16), values, preferred_element_type=jnp.float32
    )
    return (row_top, totals, summed)


def local(q_new, kv_new, kv_cache, page_table, block_offsets):
    q_rows = q_new.shape[0]
    kv_heads = kv_new.shape[1]
    head_size = kv_new.shape[2] // 2
    group_size = q_new.shape[1] // (head_size * kv_heads)
    slots_dev = kv_cache.shape[0]
    page_len = kv_cache.shape[2]
    npages = page_table.shape[0]
    blocks = lax.axis_size("blk")
    myself = lax.axis_index("blk")
    pg = -(-npages // blocks)
    block_ids = jnp.arange(blocks, dtype=jnp.int32)
    my_offset = jnp.sum(jnp.where(block_ids == myself, block_offsets, 0))
    query_pos = jnp.tile(my_offset * q_rows + jnp.arange(q_rows, dtype=jnp.int32), group_size)
    queries = (
        q_new.reshape(q_rows, kv_heads, group_size, head_size)
        .transpose(1, 2, 0, 3)
        .reshape(kv_heads, group_size * q_rows, head_size)
    )
    query_span = group_size * q_rows
    page_owner = page_table // slots_dev
    owned = page_owner == myself
    page_rank = jnp.cumsum(owned.astype(jnp.int32)) - 1
    local_slot = page_table % slots_dev
    counts = jnp.sum((page_owner[None, :] == block_ids[:, None]).astype(jnp.int32), axis=1)
    per_peer = (CAP + blocks - 1) // blocks
    starts = jnp.cumsum(counts) - counts
    my_start = jnp.sum(jnp.where(block_ids == myself, starts, 0))
    peer_slots = jnp.arange(per_peer, dtype=jnp.int32)[None, :]
    wanted = (block_ids[:, None] - my_start) % blocks + peer_slots * blocks
    picked = owned[None, None, :] & (page_rank[None, None, :] == wanted[..., None])
    chosen = jnp.sum(jnp.where(picked, local_slot[None, None, :], 0), axis=2).reshape(-1)
    sent_pages = kv_cache[chosen].reshape(blocks, per_peer, kv_heads, page_len, 2 * head_size)
    sent_pages = sent_pages.transpose(0, 2, 1, 3, 4).reshape(
        blocks, kv_heads, per_peer * page_len, 2 * head_size
    )
    own_rows = jnp.broadcast_to(
        kv_new.transpose(1, 0, 2)[None], (blocks, kv_heads, q_rows, 2 * head_size)
    )
    payload = jnp.concatenate([sent_pages, own_rows], axis=2)
    received = lax.all_to_all(payload, "blk", split_axis=0, concat_axis=0, tiled=True)
    page_part = received[:, :, : per_peer * page_len]
    page_part = page_part.reshape(blocks, kv_heads, per_peer, page_len, 2 * head_size)
    page_part = page_part.transpose(0, 2, 1, 3, 4).reshape(
        blocks * per_peer, kv_heads, page_len, 2 * head_size
    )
    arriving = (myself - starts[:, None]) % blocks + peer_slots * blocks
    present = (arriving < counts[:, None]).reshape(-1)
    order_rank = jnp.cumsum(present.astype(jnp.int32)) - 1
    choose = present[None, :] & (order_rank[None, :] == jnp.arange(pg, dtype=jnp.int32)[:, None])
    positions = jnp.sum(
        jnp.where(choose, jnp.arange(blocks * per_peer, dtype=jnp.int32)[None, :], 0), axis=1
    )
    compact = page_part[positions]
    compact_valid = jnp.arange(pg, dtype=jnp.int32) * blocks + myself < npages
    gathered = lax.all_gather(compact, "blk", axis=0, tiled=True)
    gathered_valid = (
        jnp.arange(pg, dtype=jnp.int32)[None, :] * blocks + block_ids[:, None] < npages
    ).reshape(-1)
    new_rows = received[:, :, per_peer * page_len :]
    new_rows = new_rows.transpose(1, 0, 2, 3).reshape(kv_heads, blocks * q_rows, 2 * head_size)
    own_pages = compact.transpose(1, 0, 2, 3).reshape(kv_heads, pg * page_len, 2 * head_size)
    entries_a = jnp.concatenate([new_rows, own_pages], axis=1)
    row_source = jnp.repeat(block_ids, q_rows)
    key_pos = jnp.sum(
        jnp.where(row_source[:, None] == block_ids[None, :], block_offsets[None, :], 0), axis=1
    ) * q_rows + jnp.tile(jnp.arange(q_rows, dtype=jnp.int32), blocks)
    visible_new = key_pos[None, :] <= query_pos[:, None]
    visible_own = jnp.broadcast_to(
        jnp.repeat(compact_valid, page_len)[None, :], (query_span, pg * page_len)
    )
    visible_a = jnp.concatenate([visible_new, visible_own], axis=1)[None]
    running = (
        jnp.full((kv_heads, query_span), -1e30, jnp.float32),
        jnp.zeros((kv_heads, query_span), jnp.float32),
        jnp.zeros((kv_heads, query_span, head_size), jnp.float32),
    )
    running = attend(
        running,
        queries,
        entries_a[..., :head_size],
        entries_a[..., head_size:],
        visible_a,
        head_size,
    )
    page_block = jnp.repeat(block_ids, pg)
    use_page = gathered_valid & (page_block != myself)
    entries_b = gathered.transpose(1, 0, 2, 3).reshape(
        kv_heads, blocks * pg * page_len, 2 * head_size
    )
    visible_b = jnp.repeat(use_page, page_len)[None, None, :]
    running = attend(
        running,
        queries,
        entries_b[..., :head_size],
        entries_b[..., head_size:],
        visible_b,
        head_size,
    )
    maxima, totals, summed = running
    attended = (summed / totals[..., None]).astype(jnp.bfloat16)
    attended = attended.reshape(kv_heads, group_size, q_rows, head_size).transpose(2, 0, 1, 3)
    return attended.reshape(q_rows, kv_heads * group_size * head_size)


def solution(mesh):
    return jax.shard_map(
        local,
        mesh=mesh,
        in_specs=(
            P(("groups", "blk"), "pool"),
            P(("groups", "blk"), "pool", None),
            P(("groups", "blk"), "pool", None, None),
            P("groups"),
            P("groups"),
        ),
        out_specs=P(("groups", "blk"), "pool"),
        check_vma=False,
    )
```

profile of v0, /device:TPU:0, one launch (start us, length us, event | category | flops | bytes accessed | tf_op | source)
XLA Modules:
  0.0 97.5 jit_solution(11759745901006424764)
XLA Ops:
  6.5 0.0 copy-start.1
  6.5 0.0 copy-start
  6.5 0.7 and_select_fusion.3
  7.3 0.7 convert_bitcast_fusion
  7.9 0.2 reduce-window.21
  8.1 0.1 convert_reduce_fusion
  8.2 0.2 reduce-window.22
  8.4 1.4 %fusion.35 = (s32[]{:T(128)}, s32[]{:T(128)}) fusion(s32[4]{0:T(128)} %param.9, s32[]{:T(128)S(6)} %axis_index.15, s32[4]{0:T(128)S(1)} %convert_reduce_fusion, s32[4,1]{0,1:T(1,128)S(1)} %reduce-window.22), kind=kLoop, calls=%fused_computation.78 | loop fusion | flops 22 | bytes 60 | tf_op jit(solution)/shard_map/reduce_sum | solution.py:39
  9.8 0.7 and_select_fusion.4
  10.5 0.2 select_reduce_fusion.1
  10.7 0.9 copy.22
  11.6 2.8 %gather_fusion = bf16[4,2,128,256]{3,2,1,0:T(8,128)(2,1)S(1)} fusion(bf16[32,2,128,256]{3,2,1,0:T(8,128)(2,1)} %param.7, s32[1024]{0:T(1024)S(1)} %pad_clamp_fusion.1), kind=kCustom, calls=%fused_computation | custom fusion | bytes 1048592 | tf_op jit(solution)/shard_map/gather | solution.py:59
  14.4 1.1 %pad_maximum_fusion = bf16[4,2,256,256]{3,2,1,0:T(8,128)(2,1)} fusion(bf16[4,2,128,256]{3,2,1,0:T(8,128)(2,1)S(1)} %broadcast_in_dim.150, bf16[4,2,128,256]{3,2,1,0:T(8,128)(2,1)S(1)} %gather_fusion), kind=kLoop, calls=%fused_computation.23 | loop fusion | flops 2097152 | bytes 2097152 | tf_op jit(solution)/shard_map/concatenate | solution.py:66
  15.5 6.3 %all-to-all-start = ((bf16[4,2,256,256]{3,2,1,0:T(8,128)(2,1)}), bf16[4,2,256,256]{3,2,1,0:T(8,128)(2,1)S(1)}, u32[]{:S(2)}, u32[]{:S(2)}) async-start(bf16[4,2,256,256]{3,2,1,0:T(8,128)(2,1)} %pad_maximum_fusion), calls=%async_computation | async-start | bytes 2097152 | tf_op jit(solution)/shard_map/all_to_all | solution.py:67
  21.8 0.0 all-gather.3.cloned.1.call-start
  21.9 0.1 and.99
  21.9 0.2 reduce-window.23
  22.1 0.0 copy-done
  22.1 0.1 copy.32
  22.2 0.1 copy.25
  22.4 0.1 broadcast_bitcast_fusion.2
  23.2 0.1 fusion.33
  23.3 0.0 copy-done.1
  23.3 0.1 select_reduce_fusion
  23.4 24.1 %all-to-all-done = bf16[4,2,256,256]{3,2,1,0:T(8,128)(2,1)S(1)} async-done(((bf16[4,2,256,256]{3,2,1,0:T(8,128)(2,1)}), bf16[4,2,256,256]{3,2,1,0:T(8,128)(2,1)S(1)}, u32[]{:S(2)}, u32[]{:S(2)}) %all-to-all-start) | async-done | bytes 1048608 | tf_op jit(solution)/shard_map/all_to_all | solution.py:67
  47.6 0.1 fusion.51
  47.7 1.3 %gather_fusion.1 = bf16[2,2,128,256]{3,2,1,0:T(8,128)(2,1)} fusion(bf16[4,2,128,256]{3,2,1,0:T(8,128)(2,1)S(1)} %get-tuple-element.10, s32[1024]{0:T(1024)S(1)} %pad_clamp_fusion), kind=kCustom, calls=%fused_computation.1 | custom fusion | bytes 524296 | tf_op jit(solution)/shard_map/gather | solution.py:80
  48.9 0.0 all-gather.3.cloned.1.call-update
  48.9 0.1 broadcast_bitcast_fusion.1
  49.0 0.4 broadcast_compare_fusion
  49.4 0.4 pad_add_fusion
  49.8 1.0 copy.24
  50.8 4.0 %fusion.4 = (f32[2,1024]{1,0:T(2,128)S(1)}, f32[2,768,1024]{2,1,0:T(8,128)}) fusion(pred[1024,768]{0,1:T(8,128)(4,1)S(1)} %pad_add_fusion, bf16[2,1024,128]{2,1,0:T(8,128)(2,1)S(1)} %bitcast.92, bf16[2,512,256]{2,1,0:T(8,128)(2,1)S(1)} %bitcast.98, bf16[2,256,256]{2,1,0:T(8,128)(2,1)S(1)} %bitcast.101), kind=kOutput, calls=%fused_computation.11 | convolution fusion | flops 408156160 | bytes 8396800 | tf_op jit(solution)/shard_map/gqd,gkd->gqk/dot_general | solution.py:14
  54.9 21.3 %all-gather.3.cloned.1.call-done = bf16[8,2,128,256]{3,2,1,0:T(8,128)(2,1)} async-done(((bf16[2,2,128,256]{3,2,1,0:T(8,128)(2,1)}), bf16[8,2,128,256]{3,2,1,0:T(8,128)(2,1)}) %all-gather.3.cloned.1.call-update) | async-done | bytes 1048592 | tf_op jit(solution)/shard_map/all_gather | solution.py:82
  76.1 1.3 %copy.27 = bf16[2,8,128,256]{3,2,1,0:T(8,128)(2,1)S(1)} copy(bf16[2,8,128,256]{3,2,0,1:T(8,128)(2,1)} %bitcast.96) | data formatting | bytes 2097152 | tf_op jit(solution)/shard_map/transpose | solution.py:114
  77.4 0.0 slice-start
  77.4 0.0 slice-start.1
  77.5 1.9 %bitcast_reduce_fusion = (f32[2,1024]{1,0:T(2,128)S(1)}, f32[2,1024,1024]{2,1,0:T(8,128)S(1)}) fusion(pred[1024]{0:T(1024)(128)(4,1)S(1)} %broadcast_bitcast_fusion.1, bf16[2,1024,128]{2,1,0:T(8,128)(2,1)S(1)} %bitcast.93, bf16[2,1024,256]{2,1,0:T(8,128)(2,1)S(1)} %bitcast.89), kind=kOutput, calls=%fused_computation.3 | convolution fusion | flops 543160320 | bytes 9446400 | tf_op jit(solution)/shard_map/gqd,gkd->gqk/dot_general | solution.py:14
  79.4 2.5 %fusion.2 = f32[2,1024]{1,0:T(2,128)S(1)} fusion(f32[2,1024,1024]{2,1,0:T(8,128)S(1)} %get-tuple-element.18, f32[2,1024]{1,0:T(2,128)S(1)} %get-tuple-element.13, pred[1024]{0:T(1024)(128)(4,1)S(1)} %broadcast_bitcast_fusion.1), kind=kLoop, calls=%fused_computation.9 | loop fusion | flops 10483712 | bytes 8406016 | tf_op jit(solution)/shard_map/reduce_sum | solution.py:20
  81.9 0.0 slice-done
  81.9 0.0 slice-done.1
  81.9 1.7 %fusion.5 = f32[2,1024]{1,0:T(2,128)S(1)} fusion(f32[2,768,1024]{2,1,0:T(8,128)S(1)} %bitcast.88, f32[2,1024]{1,0:T(2,128)S(1)} %get-tuple-element.14, pred[1024,768]{0,1:T(8,128)(4,1)S(1)} %pad_add_fusion), kind=kLoop, calls=%fused_computation.12 | loop fusion | flops 7862272 | bytes 7094272 | tf_op jit(solution)/shard_map/reduce_sum | solution.py:20
  83.6 2.8 %fusion.20 = f32[2,1024,128]{2,1,0:T(8,128)S(1)} fusion(f32[2,768,1024]{2,1,0:T(8,128)S(1)} %bitcast.88, f32[2,1024]{1,0:T(2,128)S(1)} %get-tuple-element.14, pred[1024,768]{0,1:T(8,128)(4,1)S(1)} %pad_add_fusion, f32[2,1024]{1,0:T(2,128)S(1)} %get-tuple-element.6, f32[2,1024]{1,0:T(2,128)S(1)} %get-tuple-element.12, ...), kind=kOutput, calls=%fused_computation.22 | convolution fusion | flops 411828224 | bytes 8937472 | tf_op jit(solution)/shard_map/gqk,gkd->gqd/dot_general | solution.py:21
  86.4 3.0 %divide_convert_fusion = bf16[2,1024,128]{2,1,0:T(8,128)(2,1)S(1)} fusion(f32[2,1024,128]{2,1,0:T(8,128)S(1)} %fusion.20, f32[2,1024,1024]{2,1,0:T(8,128)S(1)} %get-tuple-element.18, f32[2,1024]{1,0:T(2,128)S(1)} %get-tuple-element.13, pred[1024]{0:T(1024)(128)(4,1)S(1)} %broadcast_bitcast_fusion.1, bf16[2,1024,256]{2,1,0:T(8,128)(2,1)S(1)} %bitcast.90, ...), kind=kOutput, calls=%fused_computation.24 | convolution fusion | flops 548143104 | bytes 10504192 | tf_op jit(solution)/shard_map/gqk,gkd->gqd/dot_general | solution.py:21
  89.4 0.3 copy.29
  89.8 0.9 copy.35
  (21 shorter events, 0.2 us)
Async XLA Ops:
  6.5 16.8 %copy-start.1 = (s32[4]{0:T(128)S(1)}, s32[4]{0:T(128)}, u32[]{:S(2)}) copy-start(s32[4]{0:T(128)} %param.9) | copy-start | bytes 52
  6.5 15.6 %copy-start = (bf16[128,2048]{1,0:T(8,128)(2,1)S(1)}, bf16[128,2048]{1,0:T(8,128)(2,1)}, u32[]{:S(2)}) copy-start(bf16[128,2048]{1,0:T(8,128)(2,1)} %param.5) | copy-start | bytes 1572868
  15.5 32.0 %all-to-all-start = ((bf16[4,2,256,256]{3,2,1,0:T(8,128)(2,1)}), bf16[4,2,256,256]{3,2,1,0:T(8,128)(2,1)S(1)}, u32[]{:S(2)}, u32[]{:S(2)}) async-start(bf16[4,2,256,256]{3,2,1,0:T(8,128)(2,1)} %pad_maximum_fusion), calls=%async_computation | async-start | bytes 2097152 | tf_op jit(solution)/shard_map/all_to_all | solution.py:67
  21.8 54.3 %all-gather.3.cloned.1.call-start = ((), (), s32[]{:S(2)}) async-start(), calls=%async_computation.1 | async-start | bytes 1310720 | tf_op jit(solution)/shard_map/all_gather | solution.py:82
  77.4 4.5 %slice-start = ((s8[6291456]{0:T(1024)(128)(4,1)}), s8[4194304]{0:T(1024)(128)(4,1)S(1)}, s32[]{:S(2)}) async-start(s8[6291456]{0:T(1024)(128)(4,1)} %bitcast.87), calls=%async_computation.2 | async-start | bytes 8388608
  77.4 4.5 %slice-start.1 = ((s8[6291456]{0:T(1024)(128)(4,1)}), s8[2097152]{0:T(1024)(128)(4,1)S(1)}, s32[]{:S(2)}) async-start(s8[6291456]{0:T(1024)(128)(4,1)} %bitcast.87), calls=%async_computation.3 | async-start | bytes 4194304
Sparse Core Ops, SparseCore 0:
  49.1 27.0 all-gather.2
where the time goes:
time: 97.9 us; the launch traced here: 97.5 us
  waiting for transfers between devices  45.4 us (46%)
  between operations  14.3 us (15%)
  matrix products  11.7 us (12%)
  other arithmetic  10.6 us (11%)
  local copies, waits for them, and re-layouts  9.17 us (9%)
  starting transfers between devices  6.32 us (6%)
    all_to_all x1, waiting for transfers between devices, local(): lax.all_to_all(payload, 'blk', split_axis=0, concat_axis=0, tiled=True)  24.1 us
    all_gather x1, waiting for transfers between devices, local(): gathered = lax.all_gather(compact, 'blk', axis=0, tiled=True)  21.3 us
    all_to_all x1, starting transfers between devices, local(): lax.all_to_all(payload, 'blk', split_axis=0, concat_axis=0, tiled=True)  6.32 us
    dot_general x2, matrix products, attend(): jnp.einsum('gqd,gkd->gqk', queries, keys, preferred_element_type=jnp.floa...  5.92 us
    dot_general x2, matrix products, attend(): jnp.einsum('gqk,gkd->gqd', weights.astype(jnp.bfloat16), values, preferre...  5.81 us
    reduce_sum x2, other arithmetic, attend(): totals = totals * factor + jnp.sum(weights, axis=2)  4.16 us
    gather x1, local copies, waits for them, and re-layouts, local(): kv_cache[chosen]  2.77 us
  transfers between devices with their start and end apart: 2, of which 2 were waited for; matrix products, arithmetic and copies ran while one was open for 7% of the time, Pallas kernels for 0%

commit v1 on v0

--- a/solution.py
+++ b/solution.py
@@ -79,7 +79,21 @@
     )
     compact = page_part[positions]
     compact_valid = jnp.arange(pg, dtype=jnp.int32) * blocks + myself < npages
-    gathered = lax.all_gather(compact, "blk", axis=0, tiled=True)
+    ways, here, step = (lax.axis_size("blk"), lax.axis_index("blk"), compact.shape[0])
+    dims = [n * ways if d == 0 else n for d, n in enumerate(compact.shape)]
+    full = lax.dynamic_update_slice_in_dim(
+        jnp.zeros(dims, compact.dtype), compact, here * step, axis=0
+    )
+    going_up = going_down = compact
+    for far in range(1, ways // 2 + 1):
+        going_up = lax.ppermute(going_up, "blk", [(d, (d + 1) % ways) for d in range(ways)])
+        full = lax.dynamic_update_slice_in_dim(full, going_up, (here - far) % ways * step, axis=0)
+        if 2 * far < ways:
+            going_down = lax.ppermute(going_down, "blk", [(d, (d - 1) % ways) for d in range(ways)])
+            full = lax.dynamic_update_slice_in_dim(
+                full, going_down, (here + far) % ways * step, axis=0
+            )
+    gathered = full
     gathered_valid = (
         jnp.arange(pg, dtype=jnp.int32)[None, :] * blocks + block_ids[:, None] < npages
     ).reshape(-1)

time: 97.9 us -> 75.9 us (0.78)
  between operations: 14.3 us -> 0.95 us
  waiting for transfers between devices: 45.4 us -> 38.1 us
  starting transfers between devices: 6.32 us -> 10.2 us
  matrix products: 11.7 us -> 8.89 us
  local copies, waits for them, and re-layouts: 9.17 us -> 6.4 us
    all_gather x1 -> x0, waiting for transfers between devices: 21.3 us -> none  [local(): gathered = lax.all_gather(compact, 'blk', axis=0, tiled=True)]
    ppermute x0 -> x3, waiting for transfers between devices: none -> 14.9 us  [the longest x2 12.8 us: local(): lax.ppermute(going_up, 'blk', [(d, (d + 1) % ways) for d in range(ways)])]
    ppermute x0 -> x3, starting transfers between devices: none -> 3.87 us  [the longest x1 3.81 us: local(): lax.ppermute(going_down, 'blk', [(d, (d - 1) % ways) for d in range(ways)])]
    dot_general x2, matrix products: 5.92 us -> 3.1 us  [attend(): jnp.einsum('gqd,gkd->gqk', queries, keys, preferred_element_type=jnp.floa...]
    select_n x1, other arithmetic: 0.7 us -> 2.01 us  [local(): wanted = (block_ids[:, None] - my_start) % blocks + peer_slots * blocks]
    transpose x1 -> x0, local copies, waits for them, and re-layouts: 1.29 us -> none  [local(): gathered.transpose(1, 0, 2, 3)]
  transfers between devices with their start and end apart: 2 -> 4, of which waited for: 2 -> 4; matrix products, arithmetic and copies ran while one was open for 7% -> 4% of each run, Pallas kernels for 0% -> 0%
where the time goes in v1:
time: 75.9 us; the launch traced here: 75.7 us
  waiting for transfers between devices  38.1 us (50%)
  other arithmetic  11.2 us (15%)
  starting transfers between devices  10.2 us (13%)
  matrix products  8.89 us (12%)
  local copies, waits for them, and re-layouts  6.4 us (8%)
  between operations  0.95 us (1%)
    all_to_all x1, waiting for transfers between devices, local(): lax.all_to_all(payload, 'blk', split_axis=0, concat_axis=0, tiled=True)  23.2 us
    ppermute x2, waiting for transfers between devices, local(): lax.ppermute(going_up, 'blk', [(d, (d + 1) % ways) for d in range(ways)])  12.8 us
    all_to_all x1, starting transfers between devices, local(): lax.all_to_all(payload, 'blk', split_axis=0, concat_axis=0, tiled=True)  6.32 us
    dot_general x2, matrix products, attend(): jnp.einsum('gqk,gkd->gqd', weights.astype(jnp.bfloat16), values, preferre...  5.79 us
    reduce_sum x2, other arithmetic, attend(): totals = totals * factor + jnp.sum(weights, axis=2)  4.12 us
    ppermute x1, starting transfers between devices, local(): lax.ppermute(going_down, 'blk', [(d, (d - 1) % ways) for d in range(ways)])  3.81 us
    dot_general x2, matrix products, attend(): jnp.einsum('gqd,gkd->gqk', queries, keys, preferred_element_type=jnp.floa...  3.1 us
    gather x1, local copies, waits for them, and re-layouts, local(): kv_cache[chosen]  2.77 us
  transfers between devices with their start and end apart: 4, of which 4 were waited for; matrix products, arithmetic and copies ran while one was open for 4% of the time, Pallas kernels for 0%

profile of v1, /device:TPU:0, one launch (start us, length us, event | category | flops | bytes accessed | tf_op | source)
XLA Modules:
  0.0 75.7 jit_solution(14516020960253932291)
XLA Ops:
  0.0 0.0 copy-start.1
  0.0 0.0 copy-start
  0.0 0.7 and_select_fusion.3
  0.7 0.7 convert_bitcast_fusion
  1.4 0.2 reduce-window.21
  1.6 0.1 convert_reduce_fusion
  1.7 0.2 reduce-window.22
  1.9 0.6 fusion.36
  2.5 2.0 %and_select_fusion.4 = (s32[4]{0:T(128)S(1)}, s32[]{:T(128)}) fusion(s32[]{:T(128)} %fusion.36, s32[4]{0:T(128)} %param.9, s32[]{:T(128)S(6)} %axis_index.19), kind=kLoop, calls=%fused_computation.71 | loop fusion | flops 59 | bytes 44 | tf_op jit(solution)/shard_map/jit(remainder)/select_n | solution.py:56
  4.5 0.2 select_reduce_fusion.1
  4.7 0.9 %copy.17 = bf16[2,128,256]{2,1,0:T(8,128)(2,1)S(1)} copy(bf16[2,128,256]{2,0,1:T(2,128)(2,1)} %bitcast.101) | data formatting | bytes 262144 | tf_op jit(solution)/shard_map/transpose | solution.py:64
  5.7 2.8 %gather_fusion = bf16[4,2,128,256]{3,2,1,0:T(8,128)(2,1)S(1)} fusion(bf16[32,2,128,256]{3,2,1,0:T(8,128)(2,1)} %param.7, s32[1024]{0:T(1024)S(1)} %pad_clamp_fusion.1), kind=kCustom, calls=%fused_computation | custom fusion | bytes 1048592 | tf_op jit(solution)/shard_map/gather | solution.py:59
  8.5 1.1 %pad_maximum_fusion = bf16[4,2,256,256]{3,2,1,0:T(8,128)(2,1)} fusion(bf16[4,2,128,256]{3,2,1,0:T(8,128)(2,1)S(1)} %broadcast_in_dim.153, bf16[4,2,128,256]{3,2,1,0:T(8,128)(2,1)S(1)} %gather_fusion), kind=kLoop, calls=%fused_computation.23 | loop fusion | flops 2097152 | bytes 2097152 | tf_op jit(solution)/shard_map/concatenate | solution.py:66
  9.5 6.3 %all-to-all-start = ((bf16[4,2,256,256]{3,2,1,0:T(8,128)(2,1)}), bf16[4,2,256,256]{3,2,1,0:T(8,128)(2,1)S(1)}, u32[]{:S(2)}, u32[]{:S(2)}) async-start(bf16[4,2,256,256]{3,2,1,0:T(8,128)(2,1)} %pad_maximum_fusion), calls=%async_computation | async-start | bytes 2097152 | tf_op jit(solution)/shard_map/all_to_all | solution.py:67
  15.9 0.1 broadcast_bitcast_fusion.2
  16.0 0.1 and.112
  16.1 0.2 reduce-window.23
  17.0 0.0 copy-done
  17.0 0.1 copy.30
  17.1 0.1 copy.20
  17.3 0.1 fusion.33
  17.4 0.0 copy-done.1
  17.4 0.1 select_reduce_fusion
  17.5 0.1 broadcast_bitcast_fusion.1
  17.6 0.4 broadcast_compare_fusion
  18.0 0.4 pad_add_fusion
  18.4 23.2 %all-to-all-done = bf16[4,2,256,256]{3,2,1,0:T(8,128)(2,1)S(1)} async-done(((bf16[4,2,256,256]{3,2,1,0:T(8,128)(2,1)}), bf16[4,2,256,256]{3,2,1,0:T(8,128)(2,1)S(1)}, u32[]{:S(2)}, u32[]{:S(2)}) %all-to-all-start) | async-done | bytes 1048608 | tf_op jit(solution)/shard_map/all_to_all | solution.py:67
  41.6 0.1 fusion.51
  41.7 0.6 gather_fusion.1
  42.3 0.1 collective-permute-start
  42.3 3.8 %collective-permute-start.1 = (bf16[2,2,128,256]{3,2,1,0:T(8,128)(2,1)S(1)}, bf16[2,2,128,256]{3,2,1,0:T(8,128)(2,1)S(1)}, u32[]{:S(2)}, u32[]{:S(2)}) collective-permute-start(bf16[2,2,128,256]{3,2,1,0:T(8,128)(2,1)S(1)} %gather_fusion.1), channel_id=1, source_target_pairs={{0,12},{4,0},{8,4},{12,8},{1,13},{5,1},{9,5},{13,9},{2,14},{6,2},{... | collective-permute-start | bytes 786440 | tf_op jit(solution)/shard_map/ppermute | solution.py:92
  46.2 1.4 %fusion.4 = (f32[2,1024]{1,0:T(2,128)S(1)}, f32[2,768,1024]{2,1,0:T(8,128)S(1)}) fusion(pred[1024,768]{0,1:T(8,128)(4,1)S(1)} %pad_add_fusion, bf16[2,1024,128]{2,1,0:T(8,128)(2,1)S(1)} %bitcast.91, bf16[2,512,256]{2,1,0:T(8,128)(2,1)S(1)} %bitcast.96, bf16[2,256,256]{2,1,0:T(8,128)(2,1)S(1)} %bitcast.99), kind=kOutput, calls=%fused_computation.11 | convolution fusion | flops 408156160 | bytes 8396800 | tf_op jit(solution)/shard_map/gqd,gkd->gqk/dot_general | solution.py:14
  47.6 0.1 broadcast_in_dim.162
  47.7 5.6 %collective-permute-done = bf16[2,2,128,256]{3,2,1,0:T(8,128)(2,1)S(1)} collective-permute-done((bf16[2,2,128,256]{3,2,1,0:T(8,128)(2,1)S(1)}, bf16[2,2,128,256]{3,2,1,0:T(8,128)(2,1)S(1)}, u32[]{:S(2)}, u32[]{:S(2)}) %collective-permute-start) | collective-permute-done | bytes 262176 | tf_op jit(solution)/shard_map/ppermute | solution.py:89
  53.4 0.0 collective-permute-start.2
  53.4 2.0 %collective-permute-done.1 = bf16[2,2,128,256]{3,2,1,0:T(8,128)(2,1)S(1)} collective-permute-done((bf16[2,2,128,256]{3,2,1,0:T(8,128)(2,1)S(1)}, bf16[2,2,128,256]{3,2,1,0:T(8,128)(2,1)S(1)}, u32[]{:S(2)}, u32[]{:S(2)}) %collective-permute-start.1) | collective-permute-done | bytes 262176 | tf_op jit(solution)/shard_map/ppermute | solution.py:92
  55.4 7.2 %collective-permute-done.2 = bf16[2,2,128,256]{3,2,1,0:T(8,128)(2,1)S(1)} collective-permute-done((bf16[2,2,128,256]{3,2,1,0:T(8,128)(2,1)S(1)}, bf16[2,2,128,256]{3,2,1,0:T(8,128)(2,1)S(1)}, u32[]{:S(2)}, u32[]{:S(2)}) %collective-permute-start.2) | collective-permute-done | bytes 262176 | tf_op jit(solution)/shard_map/ppermute | solution.py:89
  62.7 1.7 %bitcast_reduce_fusion = (f32[2,1024]{1,0:T(2,128)S(1)}, f32[2,1024,1024]{2,1,0:T(8,128)S(1)}) fusion(pred[1024]{0:T(1024)(128)(4,1)S(1)} %broadcast_bitcast_fusion.1, bf16[2,1024,128]{2,1,0:T(8,128)(2,1)S(1)} %bitcast.92, bf16[2,1024,256]{2,1,0:T(8,128)(2,1)S(1)} %bitcast.88), kind=kOutput, calls=%fused_computation.3 | convolution fusion | flops 543160320 | bytes 9446400 | tf_op jit(solution)/shard_map/gqd,gkd->gqk/dot_general | solution.py:14
  64.4 2.5 %fusion.2 = f32[2,1024]{1,0:T(2,128)S(1)} fusion(f32[2,1024,1024]{2,1,0:T(8,128)S(1)} %get-tuple-element.18, f32[2,1024]{1,0:T(2,128)S(1)} %get-tuple-element.13, pred[1024]{0:T(1024)(128)(4,1)S(1)} %broadcast_bitcast_fusion.1), kind=kLoop, calls=%fused_computation.9 | loop fusion | flops 10483712 | bytes 8406016 | tf_op jit(solution)/shard_map/reduce_sum | solution.py:20
  66.9 1.7 %fusion.5 = f32[2,1024]{1,0:T(2,128)S(1)} fusion(f32[2,768,1024]{2,1,0:T(8,128)S(1)} %get-tuple-element.16, f32[2,1024]{1,0:T(2,128)S(1)} %get-tuple-element.14, pred[1024,768]{0,1:T(8,128)(4,1)S(1)} %pad_add_fusion), kind=kLoop, calls=%fused_computation.12 | loop fusion | flops 7862272 | bytes 7094272 | tf_op jit(solution)/shard_map/reduce_sum | solution.py:20
  68.6 2.8 %fusion.20 = f32[2,1024,128]{2,1,0:T(8,128)S(1)} fusion(f32[2,768,1024]{2,1,0:T(8,128)S(1)} %get-tuple-element.16, f32[2,1024]{1,0:T(2,128)S(1)} %get-tuple-element.14, pred[1024,768]{0,1:T(8,128)(4,1)S(1)} %pad_add_fusion, f32[2,1024]{1,0:T(2,128)S(1)} %get-tuple-element.6, f32[2,1024]{1,0:T(2,128)S(1)} %get-tuple-element.12, ...), kind=kOutput, calls=%fused_computation.22 | convolution fusion | flops 411828224 | bytes 8937472 | tf_op jit(solution)/shard_map/gqk,gkd->gqd/dot_general | solution.py:21
  71.4 3.0 %divide_convert_fusion = bf16[2,1024,128]{2,1,0:T(8,128)(2,1)S(1)} fusion(f32[2,1024,128]{2,1,0:T(8,128)S(1)} %fusion.20, f32[2,1024,1024]{2,1,0:T(8,128)S(1)} %get-tuple-element.18, f32[2,1024]{1,0:T(2,128)S(1)} %get-tuple-element.13, pred[1024]{0:T(1024)(128)(4,1)S(1)} %broadcast_bitcast_fusion.1, bf16[2,1024,256]{2,1,0:T(8,128)(2,1)S(1)} %bitcast.89, ...), kind=kOutput, calls=%fused_computation.24 | convolution fusion | flops 548143104 | bytes 10504192 | tf_op jit(solution)/shard_map/gqk,gkd->gqd/dot_general | solution.py:21
  74.4 0.3 copy.27
  74.7 0.9 %copy.37 = bf16[16,8,16,128]{3,1,2,0:T(8,128)(2,1)} copy(bf16[16,8,16,128]{3,2,1,0:T(8,128)(2,1)S(1)} %bitcast.93) | data formatting | bytes 1048576
  (25 shorter events, 0.3 us)
Async XLA Ops:
  0.0 17.4 %copy-start.1 = (s32[4]{0:T(128)S(1)}, s32[4]{0:T(128)}, u32[]{:S(2)}) copy-start(s32[4]{0:T(128)} %param.9) | copy-start | bytes 52
  0.0 17.0 %copy-start = (bf16[128,2048]{1,0:T(8,128)(2,1)S(1)}, bf16[128,2048]{1,0:T(8,128)(2,1)}, u32[]{:S(2)}) copy-start(bf16[128,2048]{1,0:T(8,128)(2,1)} %param.5) | copy-start | bytes 1572868
  9.5 32.0 %all-to-all-start = ((bf16[4,2,256,256]{3,2,1,0:T(8,128)(2,1)}), bf16[4,2,256,256]{3,2,1,0:T(8,128)(2,1)S(1)}, u32[]{:S(2)}, u32[]{:S(2)}) async-start(bf16[4,2,256,256]{3,2,1,0:T(8,128)(2,1)} %pad_maximum_fusion), calls=%async_computation | async-start | bytes 2097152 | tf_op jit(solution)/shard_map/all_to_all | solution.py:67
  42.3 11.1 %collective-permute-start = (bf16[2,2,128,256]{3,2,1,0:T(8,128)(2,1)S(1)}, bf16[2,2,128,256]{3,2,1,0:T(8,128)(2,1)S(1)}, u32[]{:S(2)}, u32[]{:S(2)}) collective-permute-start(bf16[2,2,128,256]{3,2,1,0:T(8,128)(2,1)S(1)} %gather_fusion.1), channel_id=1, source_target_pairs={{0,4},{4,8},{8,12},{12,0},{1,5},{5,9},{9,13},{13,1},{2,6},{6,10},{... | collective-permute-start | bytes 786440 | tf_op jit(solution)/shard_map/ppermute | solution.py:89
  42.3 13.1 %collective-permute-start.1 = (bf16[2,2,128,256]{3,2,1,0:T(8,128)(2,1)S(1)}, bf16[2,2,128,256]{3,2,1,0:T(8,128)(2,1)S(1)}, u32[]{:S(2)}, u32[]{:S(2)}) collective-permute-start(bf16[2,2,128,256]{3,2,1,0:T(8,128)(2,1)S(1)} %gather_fusion.1), channel_id=1, source_target_pairs={{0,12},{4,0},{8,4},{12,8},{1,13},{5,1},{9,5},{13,9},{2,14},{6,2},{... | collective-permute-start | bytes 786440 | tf_op jit(solution)/shard_map/ppermute | solution.py:92
  53.4 9.3 %collective-permute-start.2 = (bf16[2,2,128,256]{3,2,1,0:T(8,128)(2,1)S(1)}, bf16[2,2,128,256]{3,2,1,0:T(8,128)(2,1)S(1)}, u32[]{:S(2)}, u32[]{:S(2)}) collective-permute-start(bf16[2,2,128,256]{3,2,1,0:T(8,128)(2,1)S(1)} %collective-permute-done), channel_id=1, source_target_pairs={{0,4},{4,8},{8,12},{12,0},{1,5},{5,9},{9,13},{13,1},{2,6},{6,10},{... | collective-permute-start | bytes 786440 | tf_op jit(solution)/shard_map/ppermute | solution.py:89
